TPU v7x, 512 devices: a whole 4x8x8 slice. The times are simulated.
512 devices in a mesh: rx: 8 (over y), tm: 16 (over z, core), bin: 4 (over x).
Axes of the slice: x: 4, y: 8, z: 8, core: 2. Of those that a mesh axis runs over, the one named last changes fastest.
Arguments:
- samples: bfloat16 [4, 4096, 4096], P('bin', 'tm', 'rx'), may hold values from -45 to 45, as said below
- test_matrix: bfloat16 [4, 4096, 512], P('bin', 'tm'), may hold values from -0.09375 to 0.09375
- forgetting: float32 [4, 16, 512], P('bin', 'tm'), may hold values from 0 to 1, as said below
- prior_sketch: bfloat16 [4, 4096, 512], P('bin', 'rx'), may hold values from -6 to 6
Outputs:
- basis: bfloat16 [4, 16, 4096, 512], P('bin', 'tm', 'rx')
- coefficients: float32 [4, 4096, 512], P('bin', 'tm')
Inputs may be any that keep to these rules, and one draw needn't show every extreme that they name: `samples`: real-valued data. `forgetting`: positive factors.
All inputs are finite; a program needn't handle non-finite values.
Results may differ from a plain program's by a relative error of at most 0.015.
Values may be sent and summed in bfloat16 or wider, within the bound.
No kernel may reach another device: no remote copies, remote signals or barrier semaphores. Data moves between devices by JAX's collectives and lax.ppermute only.
A program may use at most 64 MiB of HBM per device.

v0:
```python
import math
import jax
import jax.numpy as jnp
from jax import lax
from jax.sharding import PartitionSpec as P


def prefix_2(part, axis, combine, identity):
    place = lax.axis_index(axis)
    gathered = jax.tree.map(lambda a: lax.all_gather(a, axis), part)
    state = jax.tree.map(lambda a, e: jnp.zeros_like(a) + jnp.asarray(e, a.dtype), part, identity)

    def one(hop, state):
        return combine(
            state, jax.tree.map(lambda a: lax.dynamic_index_in_dim(a, hop, 0, False), gathered)
        )

    return lax.fori_loop(0, place, one, state)


def with_halo(block, sides, width):
    for axis, dim in sides:
        count = lax.axis_size(axis)
        forward = [(i, i + 1) for i in range(count - 1)]
        backward = [(target, source) for source, target in forward]
        low = lax.ppermute(
            lax.slice_in_dim(block, block.shape[dim] - width, None, axis=dim), axis, forward
        )
        high = lax.ppermute(lax.slice_in_dim(block, 0, width, axis=dim), axis, backward)
        block = jnp.concatenate([low, block, high], axis=dim)
    return block


def combine(earlier, later):
    return (earlier[0] * later[0], later[0][None, :] * earlier[1] + later[1])


def sketch_of(block_data, block_test):
    return lax.dot_general(
        block_data, block_test, (((0,), (0,)), ((), ())), preferred_element_type=jnp.float32
    )


def body(samples, test_matrix, forgetting, prior_sketch):
    block_data = samples[0]
    block_test = test_matrix[0]
    own_decay = forgetting[0, 0]
    prior_rows = prior_sketch[0].astype(jnp.float32)
    width = block_test.shape[1]
    rows = block_data.shape[1]
    sketch = sketch_of(block_data, block_test)
    identity = (jnp.ones((width,), jnp.float32), jnp.zeros((rows, width), jnp.float32))
    before_decay, before_sum = prefix_2((own_decay, sketch), "tm", combine, identity)
    prefix = (
        own_decay[None, :] * before_sum + sketch + (before_decay * own_decay)[None, :] * prior_rows
    )
    padded = with_halo(prefix[None], (("bin", 0),), 1)
    mixed = padded[1] + 0.25 * (padded[0] + padded[2])
    local_gram = lax.dot_general(
        mixed,
        mixed,
        (((0,), (0,)), ((), ())),
        precision=lax.Precision.HIGHEST,
        preferred_element_type=jnp.float32,
    )
    gram = lax.psum(local_gram, "rx")
    factor = jnp.linalg.cholesky(gram)
    ortho = jax.scipy.linalg.solve_triangular(factor, mixed.T, lower=True).T
    local_coords = jnp.dot(
        block_data.astype(jnp.float32),
        ortho,
        precision=lax.Precision.HIGHEST,
        preferred_element_type=jnp.float32,
    )
    coords = lax.psum(local_coords.astype(jnp.bfloat16), "rx").astype(jnp.float32)
    receivers = rows * lax.axis_size("rx")
    basis = (math.sqrt(receivers) * ortho).astype(jnp.bfloat16)
    return (basis[None, None], coords[None])


def solution(mesh):
    return jax.shard_map(
        body,
        mesh=mesh,
        in_specs=(
            P("bin", "tm", "rx"),
            P("bin", "tm", None),
            P("bin", "tm", None),
            P("bin", "rx", None),
        ),
        out_specs=(P("bin", "tm", "rx", None), P("bin", "tm", None)),
        check_vma=False,
    )
```

profile of v0, /device:TPU:2, one launch (start us, length us, event | category | flops | bytes accessed | tf_op | source)
XLA Modules:
  0.0 489.7 jit_solution(11235781154400756800)
XLA Ops:
  7.2 0.9 copy-done
  8.1 2.3 fusion.15
  10.5 23.6 %all-gather = f32[16,1,512]{2,1,0:T(1,128)S(1)} all-gather(f32[1,1,512]{2,1,0:T(1,128)} %param.8), channel_id=2, replica_groups=mesh['rx'=8,'tm'=16,'bin'=4] {'tm'}, dimensions={0}, use_global_device_ids=true | all-gather | bytes 34816 | tf_op jit(solution)/shard_map/all_gather | solution.py:10
  34.1 79.9 %all-gather.4.cloned.1.call-done = f32[8192,512]{1,0:T(8,128)} async-done(((f32[512,512]{1,0:T(8,128)}), f32[8192,512]{1,0:T(8,128)}) %all-gather.4.cloned.1.call-update) | async-done | bytes 16777232 | tf_op jit(solution)/shard_map/all_gather | solution.py:10
  114.5 3.4 collective-permute-start
  117.9 2.5 collective-permute-start.1
  120.4 21.0 %collective-permute-done = f32[1,512,512]{2,1,0:T(8,128)S(1)} collective-permute-done((f32[1,512,512]{2,1,0:T(8,128)S(1)}, f32[1,512,512]{2,1,0:T(8,128)S(1)}, u32[]{:S(2)}, u32[]{:S(2)}) %collective-permute-start) | collective-permute-done | bytes 1048608 | tf_op jit(solution)/shard_map/ppermute | solution.py:26
  141.4 3.7 collective-permute-done.1
  145.1 1.6 bitcast_add_fusion.2
  146.7 2.9 fusion.40
  149.6 0.5 all-reduce.6.cloned.1.call-start
  150.1 101.0 %all-reduce.4.cloned.1.call-done = f32[512,512]{0,1:T(8,128)} async-done(((f32[512,512]{0,1:T(8,128)}), f32[512,512]{0,1:T(8,128)}) %all-reduce.4.cloned.1.call-update) | async-done | bytes 1048592 | tf_op jit(solution)/shard_map/psum | solution.py:66
  251.1 1.6 copy.12
  252.7 1.4 fusion.2
  254.2 11.7 %cholesky.103 = f32[128,128]{1,0:T(8,128)S(1)} custom-call(f32[128,128]{1,0:T(8,128)S(1)} %cholesky.263), custom_call_target="Cholesky" | custom-call | tf_op jit(solution)/shard_map/jit(cholesky)/cholesky | solution.py:67
  266.0 9.8 %custom-call.31 = f32[1,128,128]{1,2,0:T(8,128)S(1)} custom-call(f32[1,128,128]{2,1,0:T(8,128)S(1)} %get-tuple-element.81), custom_call_target="InvertDiagBlocksLowerTriangular" | custom-call | tf_op jit(solution)/shard_map/jit(cholesky)/cholesky | solution.py:67
  276.5 0.7 copy-done.3
  277.2 11.7 %cholesky.215 = f32[128,128]{1,0:T(8,128)S(1)} custom-call(f32[128,128]{1,0:T(8,128)S(1)} %cholesky.267), custom_call_target="Cholesky" | custom-call | tf_op jit(solution)/shard_map/jit(cholesky)/cholesky | solution.py:67
  288.9 10.0 %custom-call.32 = f32[1,128,128]{1,2,0:T(8,128)S(1)} custom-call(f32[1,128,128]{2,1,0:T(8,128)S(1)} %get-tuple-element.78), custom_call_target="InvertDiagBlocksLowerTriangular" | custom-call | tf_op jit(solution)/shard_map/jit(cholesky)/cholesky | solution.py:67
  298.9 1.2 convolution_dynamic-update-slice_fusion
  300.5 0.6 cholesky.272
  301.1 13.2 %cholesky.236 = f32[128,128]{1,0:T(8,128)} custom-call(f32[128,128]{1,0:T(8,128)} %cholesky.272), custom_call_target="Cholesky" | custom-call | tf_op jit(solution)/shard_map/jit(cholesky)/cholesky | solution.py:67
  314.3 1.5 select_reduce_fusion.1
  315.8 0.7 compare_reduce_fusion.1
  316.4 11.3 %custom-call.33 = f32[1,128,128]{1,2,0:T(8,128)} custom-call(f32[1,128,128]{2,1,0:T(8,128)} %get-tuple-element.75), custom_call_target="InvertDiagBlocksLowerTriangular" | custom-call | tf_op jit(solution)/shard_map/jit(cholesky)/cholesky | solution.py:67
  327.7 1.0 convolution_dynamic-update-slice_fusion.1
  329.1 11.7 %cholesky.253 = f32[128,128]{1,0:T(8,128)S(1)} custom-call(f32[128,128]{1,0:T(8,128)S(1)} %convolution_subtract_fusion.5), custom_call_target="Cholesky" | custom-call | tf_op jit(solution)/shard_map/jit(cholesky)/cholesky | solution.py:67
  340.9 0.7 compare_reduce_fusion
  341.6 0.6 compare_reduce_fusion.2
  345.1 10.9 %while.14 = (s32[]{:T(128)}, f32[512,512]{1,0:T(8,128)S(1)}, s32[4,2]{0,1:T(2,128)S(1)}, f32[4,128,128]{2,1,0:T(8,128)}, s32[]{:T(128)}) while((s32[]{:T(128)}, f32[512,512]{1,0:T(8,128)S(1)}, s32[4,2]{0,1:T(2,128)S(1)}, f32[4,128,128]{2,1,0:T(8,128)}, s32[]{:T(128)}) %tuple.49), condition=%wide.while_cond, body=%wide.while_body.sunk | while | flops 2 | bytes 132705 | solution.py:68
  345.2 0.6 fusion.49
  345.8 2.1 bitcast_dynamic-update-slice_fusion.2
  347.9 0.6 fusion.49
  348.5 2.1 bitcast_dynamic-update-slice_fusion.2
  350.6 0.6 fusion.49
  351.2 2.1 bitcast_dynamic-update-slice_fusion.2
  353.4 0.6 fusion.49
  354.0 2.1 bitcast_dynamic-update-slice_fusion.2
  356.0 40.1 %custom-call.34 = f32[4,128,128]{1,2,0:T(8,128)S(1)} custom-call(f32[4,128,128]{2,1,0:T(8,128)} %get-tuple-element.45), custom_call_target="InvertDiagBlocksLowerTriangular" | custom-call | tf_op jit(solution)/shard_map/jit(_solve_triangular)/triangular_solve | solution.py:68
  396.6 0.6 convolution_subtract_fusion.1
  397.6 1.0 convolution_subtract_fusion
  398.6 1.3 fusion.27
  399.9 1.5 convolution_subtract_fusion.2
  401.4 1.3 fusion.26
  402.6 1.3 fusion
  404.1 1.0 copy.13
  405.1 75.9 %all-reduce.6.cloned.1.call-done = bf16[1,256,512]{1,2,0:T(8,128)(2,1)} async-done(((bf16[1,256,512]{1,2,0:T(8,128)(2,1)}), bf16[1,256,512]{1,2,0:T(8,128)(2,1)}) %all-reduce.6.cloned.1.call-update) | async-done | bytes 262160 | tf_op jit(solution)/shard_map/psum | solution.py:75
  481.0 1.9 copy.14
  (42 shorter events, 3.8 us)
Async XLA Ops:
  7.2 1.0 copy-start
  7.2 107.0 %copy-start.5 = (f32[1,1,512]{2,1,0:T(1,128)S(1)}, f32[1,1,512]{2,1,0:T(1,128)}, u32[]{:S(2)}) copy-start(f32[1,1,512]{2,1,0:T(1,128)} %param.8) | copy-start | bytes 6148
  7.2 107.0 %copy-start.2 = (bf16[1,512,512]{2,1,0:T(8,128)(2,1)S(1)}, bf16[1,512,512]{2,1,0:T(8,128)(2,1)}, u32[]{:S(2)}) copy-start(bf16[1,512,512]{2,1,0:T(8,128)(2,1)} %param.9) | copy-start | bytes 1572868
  7.2 106.8 %all-gather.4.cloned.1.call-start = ((), (), s32[]{:S(2)}) async-start(), calls=%async_computation.2 | async-start | bytes 17825792 | tf_op jit(solution)/shard_map/all_gather | solution.py:10
  10.4 103.8 %copy-start.1 = (f32[512,512]{1,0:T(8,128)S(1)}, f32[512,512]{1,0:T(8,128)}, u32[]{:S(2)}) copy-start(f32[512,512]{1,0:T(8,128)} %fusion.15) | copy-start | bytes 3145732
  10.4 240.7 %all-reduce.4.cloned.1.call-start = ((), (), s32[]{:S(2)}) async-start(), calls=%async_computation | async-start | bytes 2097152 | tf_op jit(solution)/shard_map/psum | solution.py:66
  114.5 27.0 %collective-permute-start = (f32[1,512,512]{2,1,0:T(8,128)S(1)}, f32[1,512,512]{2,1,0:T(8,128)S(1)}, u32[]{:S(2)}, u32[]{:S(2)}) collective-permute-start(f32[1,512,512]{2,1,0:T(8,128)S(1)} %fusion.35), channel_id=1, source_target_pairs={{0,1},{1,2},{2,3},{4,5},{5,6},{6,7},{8,9},{9,10},{10,11},{12,13},{... | collective-permute-start | bytes 3145736 | tf_op jit(solution)/shard_map/ppermute | solution.py:26
  117.9 27.2 %collective-permute-start.1 = (f32[1,512,512]{2,1,0:T(8,128)S(1)}, f32[1,512,512]{2,1,0:T(8,128)S(1)}, u32[]{:S(2)}, u32[]{:S(2)}) collective-permute-start(f32[1,512,512]{2,1,0:T(8,128)S(1)} %fusion.35), channel_id=1, source_target_pairs={{1,0},{2,1},{3,2},{5,4},{6,5},{7,6},{9,8},{10,9},{11,10},{13,12},{... | collective-permute-start | bytes 3145736 | tf_op jit(solution)/shard_map/ppermute | solution.py:29
  149.6 331.4 %all-reduce.6.cloned.1.call-start = ((), (), s32[]{:S(2)}) async-start(), calls=%async_computation.1 | async-start | bytes 524288 | tf_op jit(solution)/shard_map/psum | solution.py:75
  276.5 0.7 copy-start.3
  396.1 1.1 copy-start.4
Sparse Core Ops, SparseCore 0:
  10.5 103.3 all-gather.3
  149.7 101.3 all-reduce.3
  404.1 76.8 all-reduce.5
where the time goes:
time: 495 us; the launch traced here: 490 us
  waiting for transfers between devices  282 us (57%)
  other arithmetic  127 us (26%)
  blocking collectives  23.6 us (5%)
  local copies, waits for them, and re-layouts  17.8 us (4%)
  between operations  16.8 us (3%)
  matrix products  16.5 us (3%)
  starting transfers between devices  6.49 us (1%)
    psum x1, waiting for transfers between devices, body(): gram = lax.psum(local_gram, 'rx')  101 us
    another operation x14, other arithmetic, body(): factor = jnp.linalg.cholesky(gram)  82.9 us
    all_gather x1, waiting for transfers between devices, prefix_2(): gathered = jax.tree.map(lambda a: lax.all_gather(a, axis), part)  79.9 us
    psum x1, waiting for transfers between devices, body(): lax.psum(local_coords.astype(jnp.bfloat16), 'rx').astype(jnp.float32)  75.9 us
    another operation x3, other arithmetic, body(): ortho = jax.scipy.linalg.solve_triangular(factor, mixed.T, lower=True).T  40.4 us
    all_gather x1, blocking collectives, prefix_2(): gathered = jax.tree.map(lambda a: lax.all_gather(a, axis), part)  23.6 us
    ppermute x1, waiting for transfers between devices, with_halo(): lax.ppermute(lax.slice_in_dim(block, block.shape[dim] - width, None, axis...  21 us
    another operation x12, local copies, waits for them, and re-layouts  10.9 us
  transfers between devices with their start and end apart: 5, of which 5 were waited for; matrix products, arithmetic and copies ran while one was open for 0% of the time, Pallas kernels for 0%

commit v1 on v0

--- a/solution.py
+++ b/solution.py
@@ -63,7 +63,11 @@
         precision=lax.Precision.HIGHEST,
         preferred_element_type=jnp.float32,
     )
-    gram = lax.psum(local_gram, "rx")
+    size = lax.axis_size("rx")
+    gram, stride = (local_gram, 1)
+    while stride < size:
+        gram = gram + lax.ppermute(gram, "rx", [(i_2, i_2 ^ stride) for i_2 in range(size)])
+        stride = 2 * stride
     factor = jnp.linalg.cholesky(gram)
     ortho = jax.scipy.linalg.solve_triangular(factor, mixed.T, lower=True).T
     local_coords = jnp.dot(

time: 495 us -> 539 us (1.089)
  waiting for transfers between devices: 282 us -> 315 us
  starting transfers between devices: 6.49 us -> 21.6 us
    ppermute x0 -> x3, waiting for transfers between devices: none -> 116 us  [body(): lax.ppermute(gram, 'rx', [(i_2, i_2 ^ stride) for i_2 in range(size)])]
    psum x1 -> x0, waiting for transfers between devices: 101 us -> none  [body(): gram = lax.psum(local_gram, 'rx')]
    psum x1, waiting for transfers between devices: 75.9 us -> 94.3 us  [body(): lax.psum(local_coords.astype(jnp.bfloat16), 'rx').astype(jnp.float32)]
    ppermute x0 -> x3, starting transfers between devices: none -> 15.6 us  [body(): lax.ppermute(gram, 'rx', [(i_2, i_2 ^ stride) for i_2 in range(size)])]
  transfers between devices with their start and end apart: 5 -> 7, of which waited for: 5 -> 7; matrix products, arithmetic and copies ran while one was open for 0% -> 0% of each run, Pallas kernels for 0% -> 0%
where the time goes in v1:
time: 539 us; the launch traced here: 533 us
  waiting for transfers between devices  315 us (58%)
  other arithmetic  123 us (23%)
  blocking collectives  23.6 us (4%)
  starting transfers between devices  21.6 us (4%)
  matrix products  17.4 us (3%)
  between operations  17.4 us (3%)
  local copies, waits for them, and re-layouts  15.9 us (3%)
    ppermute x3, waiting for transfers between devices, body(): lax.ppermute(gram, 'rx', [(i_2, i_2 ^ stride) for i_2 in range(size)])  116 us
    psum x1, waiting for transfers between devices, body(): lax.psum(local_coords.astype(jnp.bfloat16), 'rx').astype(jnp.float32)  94.3 us
    all_gather x1, waiting for transfers between devices, prefix_2(): gathered = jax.tree.map(lambda a: lax.all_gather(a, axis), part)  79.9 us
    another operation x14, other arithmetic, body(): factor = jnp.linalg.cholesky(gram)  78.7 us
    another operation x3, other arithmetic, body(): ortho = jax.scipy.linalg.solve_triangular(factor, mixed.T, lower=True).T  40.3 us
    all_gather x1, blocking collectives, prefix_2(): gathered = jax.tree.map(lambda a: lax.all_gather(a, axis), part)  23.6 us
    ppermute x1, waiting for transfers between devices, with_halo(): lax.ppermute(lax.slice_in_dim(block, block.shape[dim] - width, None, axis...  21 us
    ppermute x3, starting transfers between devices, body(): lax.ppermute(gram, 'rx', [(i_2, i_2 ^ stride) for i_2 in range(size)])  15.6 us
  transfers between devices with their start and end apart: 7, of which 7 were waited for; matrix products, arithmetic and copies ran while one was open for 0% of the time, Pallas kernels for 0%

profile of v1, /device:TPU:2, one launch (start us, length us, event | category | flops | bytes accessed | tf_op | source)
XLA Modules:
  0.0 533.5 jit_solution(14632874524393708154)
XLA Ops:
  7.2 0.9 copy-done
  8.1 2.3 fusion.16
  10.5 23.6 %all-gather = f32[16,1,512]{2,1,0:T(1,128)S(1)} all-gather(f32[1,1,512]{2,1,0:T(1,128)} %param.8), channel_id=2, replica_groups=mesh['rx'=8,'tm'=16,'bin'=4] {'tm'}, dimensions={0}, use_global_device_ids=true | all-gather | bytes 34816 | tf_op jit(solution)/shard_map/all_gather | solution.py:10
  34.1 79.9 %all-gather.4.cloned.1.call-done = f32[8192,512]{1,0:T(8,128)} async-done(((f32[512,512]{1,0:T(8,128)}), f32[8192,512]{1,0:T(8,128)}) %all-gather.4.cloned.1.call-update) | async-done | bytes 16777232 | tf_op jit(solution)/shard_map/all_gather | solution.py:10
  114.5 3.4 collective-permute-start
  117.9 2.5 collective-permute-start.1
  120.4 21.0 %collective-permute-done = f32[1,512,512]{2,1,0:T(8,128)S(1)} collective-permute-done((f32[1,512,512]{2,1,0:T(8,128)S(1)}, f32[1,512,512]{2,1,0:T(8,128)S(1)}, u32[]{:S(2)}, u32[]{:S(2)}) %collective-permute-start) | collective-permute-done | bytes 1048608 | tf_op jit(solution)/shard_map/ppermute | solution.py:26
  141.4 3.7 collective-permute-done.1
  145.1 1.6 bitcast_add_fusion.2
  146.7 1.9 fusion.45
  148.6 3.4 collective-permute-start.2
  152.0 24.1 %collective-permute-done.2 = f32[512,512]{0,1:T(8,128)S(1)} collective-permute-done((f32[512,512]{0,1:T(8,128)S(1)}, f32[512,512]{0,1:T(8,128)S(1)}, u32[]{:S(2)}, u32[]{:S(2)}) %collective-permute-start.2) | collective-permute-done | bytes 1048608 | tf_op jit(solution)/shard_map/ppermute | solution.py:69
  176.2 4.3 collective-permute-start.3
  180.6 45.7 %collective-permute-done.3 = f32[512,512]{0,1:T(8,128)S(1)} collective-permute-done((f32[512,512]{0,1:T(8,128)S(1)}, f32[512,512]{0,1:T(8,128)S(1)}, u32[]{:S(2)}, u32[]{:S(2)}) %collective-permute-start.3) | collective-permute-done | bytes 1048608 | tf_op jit(solution)/shard_map/ppermute | solution.py:69
  226.4 7.9 %collective-permute-start.4 = (f32[512,512]{0,1:T(8,128)S(1)}, f32[512,512]{0,1:T(8,128)}, u32[]{:S(2)}, u32[]{:S(2)}) collective-permute-start(f32[512,512]{0,1:T(8,128)S(1)} %add.82), channel_id=1, source_target_pairs={{0,256},{64,320},{128,384},{192,448},{256,0},{320,64},{384,128},{4... | collective-permute-start | bytes 3145736 | tf_op jit(solution)/shard_map/ppermute | solution.py:69
  234.3 45.9 %collective-permute-done.4 = f32[512,512]{0,1:T(8,128)} collective-permute-done((f32[512,512]{0,1:T(8,128)S(1)}, f32[512,512]{0,1:T(8,128)}, u32[]{:S(2)}, u32[]{:S(2)}) %collective-permute-start.4) | collective-permute-done | bytes 1048608 | tf_op jit(solution)/shard_map/ppermute | solution.py:69
  280.2 1.4 add.83
  282.2 1.0 copy-done.2
  283.2 11.7 %cholesky.103 = f32[128,128]{1,0:T(8,128)S(1)} custom-call(f32[128,128]{1,0:T(8,128)S(1)} %cholesky.263), custom_call_target="Cholesky" | custom-call | tf_op jit(solution)/shard_map/jit(cholesky)/cholesky | solution.py:71
  295.1 9.8 %custom-call.31 = f32[1,128,128]{1,2,0:T(8,128)S(1)} custom-call(f32[1,128,128]{2,1,0:T(8,128)S(1)} %get-tuple-element.81), custom_call_target="InvertDiagBlocksLowerTriangular" | custom-call | tf_op jit(solution)/shard_map/jit(cholesky)/cholesky | solution.py:71
  304.9 1.2 constant_dynamic-update-slice_fusion.3
  306.1 1.3 slice_subtract_fusion
  307.4 11.7 %cholesky.215 = f32[128,128]{1,0:T(8,128)S(1)} custom-call(f32[128,128]{1,0:T(8,128)S(1)} %cholesky.267), custom_call_target="Cholesky" | custom-call | tf_op jit(solution)/shard_map/jit(cholesky)/cholesky | solution.py:71
  319.1 10.0 %custom-call.32 = f32[1,128,128]{1,2,0:T(8,128)S(1)} custom-call(f32[1,128,128]{2,1,0:T(8,128)S(1)} %get-tuple-element.78), custom_call_target="InvertDiagBlocksLowerTriangular" | custom-call | tf_op jit(solution)/shard_map/jit(cholesky)/cholesky | solution.py:71
  329.4 1.3 slice_subtract_fusion.1
  330.7 11.7 %cholesky.236 = f32[128,128]{1,0:T(8,128)S(1)} custom-call(f32[128,128]{1,0:T(8,128)S(1)} %cholesky.272), custom_call_target="Cholesky" | custom-call | tf_op jit(solution)/shard_map/jit(cholesky)/cholesky | solution.py:71
  342.4 0.7 compare_reduce_fusion.1
  343.1 9.8 %custom-call.33 = f32[1,128,128]{1,2,0:T(8,128)S(1)} custom-call(f32[1,128,128]{2,1,0:T(8,128)S(1)} %get-tuple-element.75), custom_call_target="InvertDiagBlocksLowerTriangular" | custom-call | tf_op jit(solution)/shard_map/jit(cholesky)/cholesky | solution.py:71
  353.2 1.2 slice_subtract_fusion.2
  354.4 11.7 %cholesky.253 = f32[128,128]{1,0:T(8,128)S(1)} custom-call(f32[128,128]{1,0:T(8,128)S(1)} %slice_subtract_fusion.2), custom_call_target="Cholesky" | custom-call | tf_op jit(solution)/shard_map/jit(cholesky)/cholesky | solution.py:71
  366.4 0.7 compare_reduce_fusion
  367.1 0.7 compare_reduce_fusion.2
  370.5 10.6 %while.14 = (s32[]{:T(128)}, f32[512,512]{1,0:T(8,128)S(1)}, s32[4,2]{0,1:T(2,128)S(1)}, f32[4,128,128]{2,1,0:T(8,128)}, s32[]{:T(128)}) while((s32[]{:T(128)}, f32[512,512]{1,0:T(8,128)S(1)}, s32[4,2]{0,1:T(2,128)S(1)}, f32[4,128,128]{2,1,0:T(8,128)}, s32[]{:T(128)}) %tuple.49), condition=%wide.while_cond, body=%wide.while_body.sunk | while | flops 2 | bytes 132705 | solution.py:72
  370.5 0.6 fusion.54
  371.1 2.0 bitcast_dynamic-update-slice_fusion.2
  373.2 0.6 fusion.54
  373.8 2.0 bitcast_dynamic-update-slice_fusion.2
  376.4 2.0 bitcast_dynamic-update-slice_fusion.2
  379.1 2.0 bitcast_dynamic-update-slice_fusion.2
  381.1 40.1 %custom-call.34 = f32[4,128,128]{1,2,0:T(8,128)S(1)} custom-call(f32[4,128,128]{2,1,0:T(8,128)} %get-tuple-element.45), custom_call_target="InvertDiagBlocksLowerTriangular" | custom-call | tf_op jit(solution)/shard_map/jit(_solve_triangular)/triangular_solve | solution.py:72
  422.7 1.0 convolution_subtract_fusion
  423.7 1.3 fusion.29
  424.9 1.5 convolution_subtract_fusion.2
  426.4 1.3 fusion.28
  427.7 1.3 fusion
  429.2 1.0 copy.15
  430.2 94.3 %all-reduce.3.cloned.1.call-done = bf16[1,256,512]{1,2,0:T(8,128)(2,1)} async-done(((bf16[1,256,512]{1,2,0:T(8,128)(2,1)}), bf16[1,256,512]{1,2,0:T(8,128)(2,1)}) %all-reduce.3.cloned.1.call-update) | async-done | bytes 262160 | tf_op jit(solution)/shard_map/psum | solution.py:79
  524.5 1.9 copy.16
  (48 shorter events, 5.5 us)
Async XLA Ops:
  7.2 1.0 copy-start
  7.2 107.0 %copy-start.5 = (f32[1,1,512]{2,1,0:T(1,128)S(1)}, f32[1,1,512]{2,1,0:T(1,128)}, u32[]{:S(2)}) copy-start(f32[1,1,512]{2,1,0:T(1,128)} %param.8) | copy-start | bytes 6148
  7.2 107.0 %copy-start.3 = (bf16[1,512,512]{2,1,0:T(8,128)(2,1)S(1)}, bf16[1,512,512]{2,1,0:T(8,128)(2,1)}, u32[]{:S(2)}) copy-start(bf16[1,512,512]{2,1,0:T(8,128)(2,1)} %param.9) | copy-start | bytes 1572868
  7.2 106.8 %all-gather.4.cloned.1.call-start = ((), (), s32[]{:S(2)}) async-start(), calls=%async_computation.1 | async-start | bytes 17825792 | tf_op jit(solution)/shard_map/all_gather | solution.py:10
  10.4 103.8 %copy-start.1 = (f32[512,512]{1,0:T(8,128)S(1)}, f32[512,512]{1,0:T(8,128)}, u32[]{:S(2)}) copy-start(f32[512,512]{1,0:T(8,128)} %fusion.16) | copy-start | bytes 3145732
  10.4 514.1 %all-reduce.3.cloned.1.call-start = ((), (), s32[]{:S(2)}) async-start(), calls=%async_computation | async-start | bytes 524288 | tf_op jit(solution)/shard_map/psum | solution.py:79
  114.5 27.0 %collective-permute-start = (f32[1,512,512]{2,1,0:T(8,128)S(1)}, f32[1,512,512]{2,1,0:T(8,128)S(1)}, u32[]{:S(2)}, u32[]{:S(2)}) collective-permute-start(f32[1,512,512]{2,1,0:T(8,128)S(1)} %fusion.40), channel_id=1, source_target_pairs={{0,1},{1,2},{2,3},{4,5},{5,6},{6,7},{8,9},{9,10},{10,11},{12,13},{... | collective-permute-start | bytes 3145736 | tf_op jit(solution)/shard_map/ppermute | solution.py:26
  117.9 27.2 %collective-permute-start.1 = (f32[1,512,512]{2,1,0:T(8,128)S(1)}, f32[1,512,512]{2,1,0:T(8,128)S(1)}, u32[]{:S(2)}, u32[]{:S(2)}) collective-permute-start(f32[1,512,512]{2,1,0:T(8,128)S(1)} %fusion.40), channel_id=1, source_target_pairs={{1,0},{2,1},{3,2},{5,4},{6,5},{7,6},{9,8},{10,9},{11,10},{13,12},{... | collective-permute-start | bytes 3145736 | tf_op jit(solution)/shard_map/ppermute | solution.py:29
  148.6 27.5 %collective-permute-start.2 = (f32[512,512]{0,1:T(8,128)S(1)}, f32[512,512]{0,1:T(8,128)S(1)}, u32[]{:S(2)}, u32[]{:S(2)}) collective-permute-start(f32[512,512]{0,1:T(8,128)S(1)} %fusion.45), channel_id=1, source_target_pairs={{0,64},{64,0},{128,192},{192,128},{256,320},{320,256},{384,448},{4... | collective-permute-start | bytes 3145736 | tf_op jit(solution)/shard_map/ppermute | solution.py:69
  176.2 50.0 %collective-permute-start.3 = (f32[512,512]{0,1:T(8,128)S(1)}, f32[512,512]{0,1:T(8,128)S(1)}, u32[]{:S(2)}, u32[]{:S(2)}) collective-permute-start(f32[512,512]{0,1:T(8,128)S(1)} %add.81), channel_id=1, source_target_pairs={{0,128},{64,192},{128,0},{192,64},{256,384},{320,448},{384,256},{4... | collective-permute-start | bytes 3145736 | tf_op jit(solution)/shard_map/ppermute | solution.py:69
  226.4 53.7 %collective-permute-start.4 = (f32[512,512]{0,1:T(8,128)S(1)}, f32[512,512]{0,1:T(8,128)}, u32[]{:S(2)}, u32[]{:S(2)}) collective-permute-start(f32[512,512]{0,1:T(8,128)S(1)} %add.82), channel_id=1, source_target_pairs={{0,256},{64,320},{128,384},{192,448},{256,0},{320,64},{384,128},{4... | collective-permute-start | bytes 3145736 | tf_op jit(solution)/shard_map/ppermute | solution.py:69
  282.2 1.0 copy-start.2
  421.2 1.1 copy-start.4
Sparse Core Ops, SparseCore 0:
  10.5 103.3 all-gather.3
  429.2 95.3 all-reduce.2
